TPU v7x, 32 devices: a whole 2x2x4 slice. The times are simulated.
32 devices in a mesh: groups: 2 (over y), frame: 4 (over x, core), row: 4 (over z).
Axes of the slice: x: 2, y: 2, z: 4, core: 2. Of those that a mesh axis runs over, the one named last changes fastest.
Arguments:
- query_in: bfloat16 [8, 4, 64, 2240], P(('groups', 'frame'), 'row'), parts along dimension 0, may hold values from -6 to 6
- key_in: bfloat16 [8, 4, 64, 2240], P(('groups', 'frame'), 'row'), parts along dimension 0, may hold values from -216 to 216
- value_in: bfloat16 [8, 4, 64, 2240], P(('groups', 'frame'), 'row'), parts along dimension 0, may hold values from -6 to 6
- stream_in: bfloat16 [8, 4, 64, 2240], P(('groups', 'frame'), 'row'), parts along dimension 0, may hold values from -6 to 6
- attn_gain: bfloat16 [2240], replicated, may hold values from 0.5 to 1.5
- ffn_gain: bfloat16 [2240], replicated, may hold values from 0.5 to 1.5
- in_weight: bfloat16 [2240, 2, 3360], P('row', None, 'frame'), may hold values from -0.125 to 0.125
- conv_weight: bfloat16 [9, 2, 3360], P(None, None, 'frame'), may hold values from -3.5 to 3.5
- out_weight: bfloat16 [3360, 2240], P('frame'), may hold values from -0.109375 to 0.109375
Outputs:
- stream_out: bfloat16 [8, 4, 64, 2240], P(('groups', 'frame'), 'row'), parts along dimension 0
- block_out: bfloat16 [8, 4, 64, 2240], P(('groups', 'frame'), 'row'), parts along dimension 0
There are 2 independent parts, one for each index of `groups`. A program takes and returns all parts, laid end to end along the dimension named above; an argument that names none is the same for every part. Nothing has to cross between parts.
All inputs are finite; a program needn't handle non-finite values.
Results may differ from a plain program's by a relative error of at most 0.01.
Values may be sent and summed in bfloat16 or wider, within the bound.
No kernel may reach another device: no remote copies, remote signals or barrier semaphores. Data moves between devices by JAX's collectives and lax.ppermute only.
A program may use at most 64 MiB of HBM per device.

v0:
```python
import jax
import jax.numpy as jnp
from jax import lax
from jax.sharding import PartitionSpec as P

HEADS = 20
HEAD_DIM = 112
NORM_EPS = 1e-06
SHARE_EPS = 1e-06


def padded_2(cells, sides, width):
    for axis, dim in sides:
        count = lax.axis_size(axis)
        ends = count - 1
        head = lax.slice_in_dim(cells, 0, width, axis=dim)
        tail = lax.slice_in_dim(cells, cells.shape[dim] - width, cells.shape[dim], axis=dim)
        cells = jnp.concatenate(
            [
                lax.ppermute(tail, axis, [(i, (i + 1) % count) for i in range(ends)]),
                cells,
                lax.ppermute(head, axis, [((i + 1) % count, i) for i in range(ends)]),
            ],
            axis=dim,
        )
    return cells


def rms_norm(features):
    return features * lax.rsqrt(jnp.mean(features * features, axis=-1, keepdims=True) + NORM_EPS)


def depthwise(padded, conv_taps, row_count, col_count, half_width):
    widened = jnp.pad(padded, ((0, 0), (0, 0), (1, 1), (0, 0)))
    summed = jnp.zeros((padded.shape[0], row_count, col_count, padded.shape[3]), jnp.float32)
    for row_off in range(3):
        for col_off in range(3):
            window = widened[
                :, row_off : row_off + row_count, col_off : col_off + col_count, :
            ].astype(jnp.float32)
            summed = summed + window * conv_taps[row_off * 3 + col_off]
    return (summed[..., :half_width] * jax.nn.silu(summed[..., half_width:])).astype(jnp.bfloat16)


def local(
    query_in, key_in, value_in, stream_in, attn_gain, ffn_gain, in_weight, conv_weight, out_weight
):
    frame_count, row_count, col_count, model_width = query_in.shape
    token_count = frame_count * row_count * col_count
    local_gated = in_weight.shape[2]
    highest = lax.Precision.HIGHEST
    key_pos = jnp.maximum(key_in, 0).reshape(token_count, HEADS, HEAD_DIM)
    value_heads = value_in.reshape(token_count, HEADS, HEAD_DIM)
    local_state = jnp.einsum(
        "thi,thj->ihj", key_pos, value_heads, preferred_element_type=jnp.float32
    ).reshape(HEAD_DIM, model_width)
    local_total = jnp.sum(key_pos.reshape(token_count, model_width), axis=0, dtype=jnp.float32)
    state_share, total_share = (
        lax.psum_scatter(
            local_state.astype(jnp.bfloat16), "row", scatter_dimension=1, tiled=True
        ).astype(jnp.float32),
        lax.psum_scatter(
            local_total.astype(jnp.bfloat16), "row", scatter_dimension=0, tiled=True
        ).astype(jnp.float32),
    )
    state_share, total_share = lax.psum((state_share, total_share), "frame")
    kv_state, key_total = (
        lax.all_gather(state_share, "row", axis=1, tiled=True),
        lax.all_gather(total_share, "row", axis=0, tiled=True),
    )
    query_pos = jnp.maximum(query_in, 0).reshape(token_count, HEADS, HEAD_DIM).astype(jnp.float32)
    numerator = jnp.einsum(
        "thi,ihj->thj", query_pos, kv_state.reshape(HEAD_DIM, HEADS, HEAD_DIM), precision=highest
    )
    denominator = jnp.einsum(
        "thi,hi->th", query_pos, key_total.reshape(HEADS, HEAD_DIM), precision=highest
    )
    attended = (numerator / (denominator[:, :, None] + SHARE_EPS)).reshape(token_count, model_width)
    stream_flat = stream_in.reshape(token_count, model_width).astype(jnp.float32)
    stream_out = (stream_flat + attn_gain.astype(jnp.float32) * rms_norm(attended)).astype(
        jnp.bfloat16
    )
    normed = (rms_norm(stream_out.astype(jnp.float32)) * ffn_gain.astype(jnp.float32)).astype(
        jnp.bfloat16
    )
    normed_grid = normed.reshape(frame_count, row_count, col_count, model_width)
    in_full = lax.all_gather(in_weight, "row", axis=0, tiled=True).reshape(
        model_width, 2 * local_gated
    )
    conv_taps = conv_weight.reshape(9, 2 * local_gated).astype(jnp.float32)
    frame_piece = lax.all_gather(normed_grid, "frame", axis=0, tiled=True)
    piece_frames = frame_piece.shape[0]
    piece_rows = frame_piece.shape[1]
    projected = jnp.dot(
        frame_piece.reshape(piece_frames * piece_rows * col_count, model_width),
        in_full,
        preferred_element_type=jnp.float32,
    )
    expanded = (
        jax.nn.silu(projected)
        .astype(jnp.bfloat16)
        .reshape(piece_frames, piece_rows, col_count, 2 * local_gated)
    )
    padded_expanded = padded_2(expanded, (("row", 1),), 1)
    hidden = depthwise(padded_expanded, conv_taps, row_count, col_count, local_gated)
    hidden_flat = hidden.reshape(-1, local_gated)
    ffn_rows = lax.psum_scatter(
        jnp.dot(hidden_flat, out_weight, preferred_element_type=jnp.float32).astype(jnp.bfloat16),
        "frame",
        scatter_dimension=0,
        tiled=True,
    ).astype(jnp.float32)
    block_out = (stream_out.astype(jnp.float32) + ffn_rows).astype(jnp.bfloat16)
    grid_shape = (frame_count, row_count, col_count, model_width)
    return (stream_out.reshape(grid_shape), block_out.reshape(grid_shape))


def solution(mesh):
    in_specs = (
        P(("groups", "frame"), "row", None, None),
        P(("groups", "frame"), "row", None, None),
        P(("groups", "frame"), "row", None, None),
        P(("groups", "frame"), "row", None, None),
        P(),
        P(),
        P("row", None, "frame"),
        P(None, None, "frame"),
        P("frame", None),
    )
    out_specs = (
        P(("groups", "frame"), "row", None, None),
        P(("groups", "frame"), "row", None, None),
    )
    return jax.shard_map(local, mesh=mesh, in_specs=in_specs, out_specs=out_specs, check_vma=False)
```

profile of v0, /device:TPU:0, one launch (start us, length us, event | category | flops | bytes accessed | tf_op | source)
XLA Modules:
  0.0 293.6 jit_solution(11495132540162727477)
XLA Ops:
  7.2 1.1 fusion.21
  8.3 0.4 reshape.204
  8.7 1.4 reshape.205
  10.1 0.4 fusion.7
  10.5 1.1 copy.25
  11.6 0.7 all-gather.5.cloned.1.call-update
  12.5 0.4 reshape.207
  12.9 0.6 fusion.25
  14.8 14.3 %all-reduce.2 = bf16[2240]{0:T(1024)(128)(2,1)S(1)} all-reduce(bf16[2240]{0:T(1024)(128)(2,1)S(1)} %get-tuple-element.8), channel_id=3, replica_groups=mesh['groups'=2,'frame'=4,'row'=4] {'row'}, use_global_device_ids=true, to_apply=%region_3.0.clone | all-reduce | flops 2240 | bytes 8960
  29.3 7.2 %reduce-scatter.3.cloned.1.call-done = bf16[112,560]{0,1:T(8,128)(2,1)} async-done(((bf16[112,2240]{0,1:T(8,128)(2,1)}), bf16[112,560]{0,1:T(8,128)(2,1)}) %reduce-scatter.3.cloned.1.call-update) | async-done | bytes 125456 | tf_op jit(solution)/shard_map/reduce_scatter | solution.py:59
  36.5 13.6 %all-reduce.5 = (f32[112,560]{0,1:T(8,128)S(1)}, f32[560]{0:T(1024)S(1)}) all-reduce(bf16[112,560]{0,1:T(8,128)(2,1)} %reduce-scatter.3.cloned.1.call-done, f32[560]{0:T(1024)S(1)} %dynamic-slice_convert_fusion), channel_id=1, replica_groups=mesh['groups'=2,'frame'=4,'row'=4] {'frame'}, use_global_device_ids=true, to_apply=%region_1.0 | all-reduce | flops 63280 | bytes 380800 | tf_op jit(solution)/shard_map/psum | solution.py:66
  50.1 0.3 dynamic-update-slice
  50.4 19.7 %all-reduce.1 = f32[2240]{0:T(1024)S(1)} all-reduce(f32[2240]{0:T(1024)S(1)} %dynamic-update-slice), channel_id=1, replica_groups=mesh['groups'=2,'frame'=4,'row'=4] {'row'}, use_global_device_ids=true, to_apply=%add.1 | all-reduce | flops 2240 | bytes 17920
  70.2 0.6 fusion.17
  70.8 42.0 %all_gather.12 = f32[112,2240]{0,1:T(8,128)S(1)} all-gather(f32[112,560]{0,1:T(8,128)S(1)} %get-tuple-element.2), channel_id=1, replica_groups=mesh['groups'=2,'frame'=4,'row'=4] {'row'}, dimensions={1}, use_global_device_ids=true | all-gather | bytes 1254400 | tf_op jit(solution)/shard_map/all_gather | solution.py:68
  112.8 1.4 multiply_reduce_fusion
  114.2 0.4 copy.28
  115.4 1.0 multiply_convert_fusion.1
  116.6 82.5 %all-gather.5.cloned.1.call-done = bf16[2240,2,840]{2,1,0:T(2,128)(2,1)} async-done(((bf16[560,2,840]{2,1,0:T(2,128)(2,1)}), bf16[2240,2,840]{2,1,0:T(2,128)(2,1)}) %all-gather.5.cloned.1.call-update) | async-done | bytes 7526416 | tf_op jit(solution)/shard_map/all_gather | solution.py:87
  199.1 22.9 %copy.30 = bf16[2240,2,840]{0,2,1:T(8,128)(2,1)} copy(bf16[2240,2,840]{2,1,0:T(2,128)(2,1)} %all-gather.5.cloned.1.call-done) | data formatting | bytes 15052800 | tf_op jit(solution)/shard_map/all_gather | solution.py:87
  221.9 5.8 %multiply_convert_fusion = bf16[256,1680]{0,1:T(8,128)(2,1)S(1)} fusion(bf16[256,2240]{1,0:T(8,128)(2,1)} %bitcast.49, bf16[2240,1680]{0,1:T(8,128)(2,1)} %bitcast.45), kind=kOutput, calls=%fused_computation.10 | convolution fusion | flops 1928908800 | bytes 9533440 | tf_op jit(solution)/shard_map/dot_general | solution.py:94
  227.8 0.6 copy.31
  228.4 1.3 collective-permute-start.1
  229.7 4.8 %collective-permute-start = (bf16[4,1,64,1680]{3,2,0,1:T(8,128)(2,1)S(1)}, bf16[4,1,64,1680]{3,2,0,1:T(8,128)(2,1)S(1)}, u32[]{:S(2)}, u32[]{:S(2)}) collective-permute-start(bf16[4,1,64,1680]{3,2,0,1:T(8,128)(2,1)S(1)} %bitcast.42), channel_id=1, source_target_pairs={{0,1},{1,2},{2,3},{4,5},{5,6},{6,7},{8,9},{9,10},{10,11},{12,13},{... | collective-permute-start | bytes 2580488 | tf_op jit(solution)/shard_map/ppermute | solution.py:20
  235.2 17.3 %collective-permute-done.1 = bf16[4,1,64,1680]{3,2,0,1:T(8,128)(2,1)S(1)} collective-permute-done((bf16[4,1,64,1680]{3,2,0,1:T(8,128)(2,1)S(1)}, bf16[4,1,64,1680]{3,2,0,1:T(8,128)(2,1)S(1)}, u32[]{:S(2)}, u32[]{:S(2)}) %collective-permute-start.1) | collective-permute-done | bytes 860192 | tf_op jit(solution)/shard_map/ppermute | solution.py:22
  252.6 1.2 collective-permute-done
  253.8 1.1 fusion.5
  254.9 1.8 multiply_add_fusion
  256.6 0.3 fusion.8
  257.0 2.4 convolution_convert_fusion
  259.4 26.0 %reduce-scatter.5.cloned.1.call-done = bf16[64,2240]{1,0:T(8,128)(2,1)} async-done(((bf16[256,2240]{1,0:T(8,128)(2,1)}), bf16[64,2240]{1,0:T(8,128)(2,1)}) %reduce-scatter.5.cloned.1.call-update) | async-done | bytes 286736 | tf_op jit(solution)/shard_map/reduce_scatter | solution.py:107
  285.4 1.7 fusion.16
  (44 shorter events, 2.0 us)
Async XLA Ops:
  7.2 29.3 %reduce-scatter.3.cloned.1.call-start = ((), (), s32[]{:S(2)}) async-start(), calls=%async_computation.2 | async-start | bytes 716800 | tf_op jit(solution)/shard_map/reduce_scatter | solution.py:59
  10.4 2.0 copy-start.3
  10.5 2.0 copy-start.4
  10.5 2.0 copy-start.1
  11.6 1.4 copy-start.5
  11.6 187.5 %all-gather.5.cloned.1.call-start = ((), (), s32[]{:S(2)}) async-start(), calls=%async_computation.4 | async-start | bytes 10035200 | tf_op jit(solution)/shard_map/all_gather | solution.py:87
  12.4 209.6 %all-gather.3.cloned.1.call-start = ((), (), s32[]{:S(2)}) async-start(), calls=%async_computation.3 | async-start | bytes 1474560 | tf_op jit(solution)/shard_map/all_gather | solution.py:91
  114.2 1.0 copy-start
  116.5 168.9 %reduce-scatter.5.cloned.1.call-start = ((), (), s32[]{:S(2)}) async-start(), calls=%async_computation.5 | async-start | bytes 1474560 | tf_op jit(solution)/shard_map/reduce_scatter | solution.py:107
  221.9 12.6 %copy-start.2 = (bf16[9,2,840]{2,1,0:T(2,128)(2,1)S(1)}, bf16[9,2,840]{2,1,0:T(2,128)(2,1)}, u32[]{:S(2)}) copy-start(bf16[9,2,840]{2,1,0:T(2,128)(2,1)} %param.16) | copy-start | bytes 90724
  228.4 24.2 %collective-permute-start.1 = (bf16[4,1,64,1680]{3,2,0,1:T(8,128)(2,1)S(1)}, bf16[4,1,64,1680]{3,2,0,1:T(8,128)(2,1)S(1)}, u32[]{:S(2)}, u32[]{:S(2)}) collective-permute-start(bf16[4,1,64,1680]{3,2,0,1:T(8,128)(2,1)S(1)} %bitcast.41), channel_id=1, source_target_pairs={{1,0},{2,1},{3,2},{5,4},{6,5},{7,6},{9,8},{10,9},{11,10},{13,12},{... | collective-permute-start | bytes 2580488 | tf_op jit(solution)/shard_map/ppermute | solution.py:22
  229.7 24.1 %collective-permute-start = (bf16[4,1,64,1680]{3,2,0,1:T(8,128)(2,1)S(1)}, bf16[4,1,64,1680]{3,2,0,1:T(8,128)(2,1)S(1)}, u32[]{:S(2)}, u32[]{:S(2)}) collective-permute-start(bf16[4,1,64,1680]{3,2,0,1:T(8,128)(2,1)S(1)} %bitcast.42), channel_id=1, source_target_pairs={{0,1},{1,2},{2,3},{4,5},{5,6},{6,7},{8,9},{9,10},{10,11},{12,13},{... | collective-permute-start | bytes 2580488 | tf_op jit(solution)/shard_map/ppermute | solution.py:20
  254.8 2.1 copy-start.6
Sparse Core Ops, SparseCore 0:
  11.7 24.6 reduce-scatter.2
  38.0 160.9 all-gather.4
  201.2 15.6 all-gather.2
  259.5 25.7 reduce-scatter.4
where the time goes:
time: 295 us; the launch traced here: 294 us
  waiting for transfers between devices  135 us (46%)
  blocking collectives  89.6 us (30%)
  local copies, waits for them, and re-layouts  29.5 us (10%)
  between operations  15.4 us (5%)
  matrix products  10.6 us (4%)
  other arithmetic  7.42 us (3%)
  starting transfers between devices  6.24 us (2%)
    all_gather x1, waiting for transfers between devices, local(): lax.all_gather(in_weight, 'row', axis=0, tiled=True)  82.5 us
    all_gather x1, blocking collectives, local(): lax.all_gather(state_share, 'row', axis=1, tiled=True)  42 us
    unnamed x2, blocking collectives  34 us
    reduce_scatter x1, waiting for transfers between devices, local(): lax.psum_scatter(jnp.dot(hidden_flat, out_weight, preferred_element_type=...  26 us
    all_gather x1, local copies, waits for them, and re-layouts, local(): lax.all_gather(in_weight, 'row', axis=0, tiled=True)  22.9 us
    ppermute x1, waiting for transfers between devices, padded_2(): lax.ppermute(head, axis, [((i + 1) % count, i) for i in range(ends)])  17.3 us
    psum x1, blocking collectives, local(): state_share, total_share = lax.psum((state_share, total_share), 'frame')  13.6 us
    reduce_scatter x1, waiting for transfers between devices, local(): lax.psum_scatter(local_state.astype(jnp.bfloat16), 'row', scatter_dimensi...  7.19 us
  transfers between devices with their start and end apart: 6, of which 5 were waited for; matrix products, arithmetic and copies ran while one was open for 10% of the time, Pallas kernels for 0%

commit v1 on v0

--- a/solution.py
+++ b/solution.py
@@ -7,6 +7,27 @@
 HEAD_DIM = 112
 NORM_EPS = 1e-06
 SHARE_EPS = 1e-06
+
+
+def laid_out(tiles, dim):
+    shape = list(tiles.shape[1:])
+    shape[dim] *= tiles.shape[0]
+    return jnp.moveaxis(tiles, 0, dim).reshape(shape)
+
+
+def grow_blocks(x, axis):
+    size, position = (lax.axis_size(axis), lax.axis_index(axis))
+    blocks, apart = (x[None], 1)
+    while apart < size:
+        other = lax.ppermute(blocks, axis, [(i, i ^ apart) for i in range(size)])
+        low = position & apart == 0
+        blocks = jnp.concatenate([jnp.where(low, blocks, other), jnp.where(low, other, blocks)])
+        apart *= 2
+    return blocks
+
+
+def collect(x, axis, dim):
+    return laid_out(grow_blocks(x, axis), dim)
 
 
 def padded_2(cells, sides, width):
@@ -84,9 +105,7 @@
         jnp.bfloat16
     )
     normed_grid = normed.reshape(frame_count, row_count, col_count, model_width)
-    in_full = lax.all_gather(in_weight, "row", axis=0, tiled=True).reshape(
-        model_width, 2 * local_gated
-    )
+    in_full = collect(in_weight, "row", 0).reshape(model_width, 2 * local_gated)
     conv_taps = conv_weight.reshape(9, 2 * local_gated).astype(jnp.float32)
     frame_piece = lax.all_gather(normed_grid, "frame", axis=0, tiled=True)
     piece_frames = frame_piece.shape[0]

time: 295 us -> 425 us (1.44)
  blocking collectives: 89.6 us -> 231 us
  waiting for transfers between devices: 135 us -> 81.3 us
  other arithmetic: 7.42 us -> 47.6 us
  starting transfers between devices: 6.24 us -> 12.3 us
  local copies, waits for them, and re-layouts: 29.5 us -> 24.2 us
    unnamed x2, blocking collectives: 34 us -> 195 us
    all_gather x1 -> x0, waiting for transfers between devices: 82.5 us -> none  [local(): lax.all_gather(in_weight, 'row', axis=0, tiled=True)]
    ppermute x0 -> x2, waiting for transfers between devices: none -> 41.2 us  [grow_blocks(): other = lax.ppermute(blocks, axis, [(i, i ^ apart) for i in range(size)])]
    all_gather x1 -> x0, local copies, waits for them, and re-layouts: 22.9 us -> none  [local(): lax.all_gather(in_weight, 'row', axis=0, tiled=True)]
    all_gather x1, blocking collectives: 42 us -> 20.4 us  [local(): lax.all_gather(state_share, 'row', axis=1, tiled=True)]
    concatenate x0 -> x2, other arithmetic: none -> 19.7 us  [grow_blocks(): jnp.concatenate([jnp.where(low, blocks, other), jnp.where(low, other, blo...]
    another operation x0 -> x1, local copies, waits for them, and re-layouts: none -> 16.9 us  [local(): in_full = collect(in_weight, 'row', 0).reshape(model_width, 2 * local_gated)]
    select_n x0 -> x2, other arithmetic: none -> 16.6 us  [grow_blocks(): jnp.where(low, blocks, other)]
  transfers between devices with their start and end apart: 6 -> 7, of which waited for: 5 -> 5; matrix products, arithmetic and copies ran while one was open for 10% -> 13% of each run, Pallas kernels for 0% -> 0%
where the time goes in v1:
time: 425 us; the launch traced here: 424 us
  blocking collectives  231 us (54%)
  waiting for transfers between devices  81.3 us (19%)
  other arithmetic  47.6 us (11%)
  local copies, waits for them, and re-layouts  24.2 us (6%)
  between operations  15.3 us (4%)
  starting transfers between devices  12.3 us (3%)
  matrix products  11.7 us (3%)
    unnamed x2, blocking collectives  195 us
    ppermute x2, waiting for transfers between devices, grow_blocks(): other = lax.ppermute(blocks, axis, [(i, i ^ apart) for i in range(size)])  41.2 us
    reduce_scatter x1, waiting for transfers between devices, local(): lax.psum_scatter(jnp.dot(hidden_flat, out_weight, preferred_element_type=...  26.4 us
    all_gather x1, blocking collectives, local(): lax.all_gather(state_share, 'row', axis=1, tiled=True)  20.4 us
    concatenate x2, other arithmetic, grow_blocks(): jnp.concatenate([jnp.where(low, blocks, other), jnp.where(low, other, blo...  19.7 us
    another operation x1, local copies, waits for them, and re-layouts, local(): in_full = collect(in_weight, 'row', 0).reshape(model_width, 2 * local_gated)  16.9 us
    select_n x2, other arithmetic, grow_blocks(): jnp.where(low, blocks, other)  16.6 us
    psum x1, blocking collectives, local(): state_share, total_share = lax.psum((state_share, total_share), 'frame')  15.6 us
  transfers between devices with their start and end apart: 7, of which 5 were waited for; matrix products, arithmetic and copies ran while one was open for 13% of the time, Pallas kernels for 0%

profile of v1, /device:TPU:0, one launch (start us, length us, event | category | flops | bytes accessed | tf_op | source)
XLA Modules:
  0.0 423.7 jit_solution(3902322712551202025)
XLA Ops:
  7.2 3.1 collective-permute-start
  10.3 1.4 reshape.202
  11.7 1.1 fusion.21
  13.2 41.2 %collective-permute-done = bf16[1,560,2,840]{3,2,1,0:T(2,128)(2,1)} collective-permute-done((bf16[1,560,2,840]{3,2,1,0:T(2,128)(2,1)}, bf16[1,560,2,840]{3,2,1,0:T(2,128)(2,1)}, u32[]{:S(2)}, u32[]{:S(2)}) %collective-permute-start) | collective-permute-done | bytes 1881632 | tf_op jit(solution)/shard_map/ppermute | solution.py:22
  54.3 5.5 %broadcast_select_fusion.3 = (bf16[1,560,2,840]{3,2,1,0:T(2,128)(2,1)S(1)}, bf16[1,560,2,840]{3,2,1,0:T(2,128)(2,1)S(1)}) fusion(bf16[1,560,2,840]{3,2,1,0:T(2,128)(2,1)} %collective-permute-done, pred[]{:T(512)S(6)} %eq.7, bf16[560,2,840]{2,1,0:T(2,128)(2,1)} %param.15), kind=kLoop, calls=%fused_computation.8 | loop fusion | flops 1881600 | bytes 7526401 | tf_op jit(solution)/shard_map/jit(_where)/select_n | solution.py:24
  59.9 7.8 %pad_maximum_fusion.1 = bf16[2,560,2,840]{3,2,1,0:T(2,128)(2,1)} fusion(bf16[1,560,2,840]{3,2,1,0:T(2,128)(2,1)S(1)} %get-tuple-element.11, bf16[1,560,2,840]{3,2,1,0:T(2,128)(2,1)S(1)} %get-tuple-element.10), kind=kLoop, calls=%fused_computation.6 | loop fusion | flops 1881600 | bytes 7526400 | tf_op jit(solution)/shard_map/concatenate | solution.py:24
  67.7 2.8 collective-permute-start.1
  70.9 1.0 copy.24
  72.2 1.0 broadcast_maximum_fusion
  75.6 96.3 %all-reduce.2 = bf16[2240]{0:T(1024)(128)(2,1)S(1)} all-reduce(bf16[2240]{0:T(1024)(128)(2,1)S(1)} %get-tuple-element.12), channel_id=3, replica_groups=mesh['groups'=2,'frame'=4,'row'=4] {'row'}, use_global_device_ids=true, to_apply=%region_3.0.clone | all-reduce | flops 2240 | bytes 8960
  171.9 0.9 reduce-scatter.3.cloned.1.call-done
  172.9 15.6 %all-reduce.5 = (f32[112,560]{0,1:T(8,128)S(1)}, f32[560]{0:T(1024)S(1)}) all-reduce(bf16[112,560]{0,1:T(8,128)(2,1)} %reduce-scatter.3.cloned.1.call-done, f32[560]{0:T(1024)S(1)} %dynamic-slice_convert_fusion), channel_id=1, replica_groups=mesh['groups'=2,'frame'=4,'row'=4] {'frame'}, use_global_device_ids=true, to_apply=%region_1.0 | all-reduce | flops 63280 | bytes 380800 | tf_op jit(solution)/shard_map/psum | solution.py:87
  188.7 99.1 %all-reduce.1 = f32[2240]{0:T(1024)S(1)} all-reduce(f32[2240]{0:T(1024)S(1)} %dynamic-update-slice), channel_id=1, replica_groups=mesh['groups'=2,'frame'=4,'row'=4] {'row'}, use_global_device_ids=true, to_apply=%add.1 | all-reduce | flops 2240 | bytes 17920
  287.9 0.6 fusion.17
  288.6 20.4 %all_gather.9 = f32[112,2240]{0,1:T(8,128)S(1)} all-gather(f32[112,560]{0,1:T(8,128)S(1)} %get-tuple-element.2), channel_id=1, replica_groups=mesh['groups'=2,'frame'=4,'row'=4] {'row'}, dimensions={1}, use_global_device_ids=true | all-gather | bytes 1254400 | tf_op jit(solution)/shard_map/all_gather | solution.py:89
  309.0 1.4 multiply_reduce_fusion
  310.8 1.0 reshape.207
  312.0 2.1 fusion.12
  314.2 2.0 multiply_convert_fusion.1
  316.3 11.1 %broadcast_select_fusion.1 = (bf16[2,560,2,840]{3,2,1,0:T(2,128)(2,1)S(1)}, bf16[2,560,2,840]{3,2,1,0:T(2,128)(2,1)S(1)}) fusion(bf16[2,560,2,840]{3,2,1,0:T(2,128)(2,1)} %collective-permute-done.1, pred[]{:T(512)S(6)} %eq.6, bf16[1,560,2,840]{3,2,1,0:T(2,128)(2,1)} %copy-done, bf16[1,560,2,840]{3,2,1,0:T(2,128)(2,1)S(1)} %get-tuple-element.10), kind=kLoop, calls=%fused_computation.4 | loop fusion | flops 5644800 | bytes 15052801 | tf_op jit(solution)/shard_map/jit(_where)/select_n | solution.py:24
  327.4 11.9 %pad_maximum_fusion = bf16[4,560,2,840]{3,2,1,0:T(2,128)(2,1)} fusion(bf16[2,560,2,840]{3,2,1,0:T(2,128)(2,1)S(1)} %get-tuple-element.9, bf16[2,560,2,840]{3,2,1,0:T(2,128)(2,1)S(1)} %get-tuple-element.8), kind=kLoop, calls=%fused_computation.2 | loop fusion | flops 3763200 | bytes 15052800 | tf_op jit(solution)/shard_map/concatenate | solution.py:24
  339.3 16.9 %reshape_reshape.4 = bf16[2240,1680]{1,0:T(8,128)(2,1)} reshape(bf16[4,560,2,840]{3,2,1,0:T(2,128)(2,1)} %pad_maximum_fusion) | data formatting | bytes 15052800 | tf_op jit(solution)/shard_map/reshape;reshape | solution.py:108
  356.2 6.9 %multiply_convert_fusion = bf16[256,1680]{0,1:T(8,128)(2,1)S(1)} fusion(bf16[256,2240]{1,0:T(8,128)(2,1)} %bitcast.51, bf16[2240,1680]{1,0:T(8,128)(2,1)} %reshape_reshape.4), kind=kOutput, calls=%fused_computation.16 | convolution fusion | flops 1928908800 | bytes 9533440 | tf_op jit(solution)/shard_map/dot_general | solution.py:113
  363.7 1.3 collective-permute-start.3
  365.0 4.8 %collective-permute-start.2 = (bf16[4,1,64,1680]{3,2,0,1:T(8,128)(2,1)S(1)}, bf16[4,1,64,1680]{3,2,0,1:T(8,128)(2,1)S(1)}, u32[]{:S(2)}, u32[]{:S(2)}) collective-permute-start(bf16[4,1,64,1680]{3,2,0,1:T(8,128)(2,1)S(1)} %bitcast.44), channel_id=1, source_target_pairs={{0,1},{1,2},{2,3},{4,5},{5,6},{6,7},{8,9},{9,10},{10,11},{12,13},{... | collective-permute-start | bytes 2580488 | tf_op jit(solution)/shard_map/ppermute | solution.py:41
  370.6 11.6 %collective-permute-done.3 = bf16[4,1,64,1680]{3,2,0,1:T(8,128)(2,1)S(1)} collective-permute-done((bf16[4,1,64,1680]{3,2,0,1:T(8,128)(2,1)S(1)}, bf16[4,1,64,1680]{3,2,0,1:T(8,128)(2,1)S(1)}, u32[]{:S(2)}, u32[]{:S(2)}) %collective-permute-start.3) | collective-permute-done | bytes 860192 | tf_op jit(solution)/shard_map/ppermute | solution.py:43
  382.2 1.2 collective-permute-done.2
  383.4 1.1 fusion.5
  384.5 1.8 multiply_add_fusion
  386.6 2.4 convolution_convert_fusion
  389.1 26.4 %reduce-scatter.5.cloned.1.call-done = bf16[64,2240]{1,0:T(8,128)(2,1)} async-done(((bf16[256,2240]{1,0:T(8,128)(2,1)}), bf16[64,2240]{1,0:T(8,128)(2,1)}) %reduce-scatter.5.cloned.1.call-update) | async-done | bytes 286736 | tf_op jit(solution)/shard_map/reduce_scatter | solution.py:126
  415.5 1.7 fusion.16
  (49 shorter events, 5.0 us)
Async XLA Ops:
  7.2 165.7 %reduce-scatter.3.cloned.1.call-start = ((), (), s32[]{:S(2)}) async-start(), calls=%async_computation.2 | async-start | bytes 716800 | tf_op jit(solution)/shard_map/reduce_scatter | solution.py:80
  7.2 47.1 %collective-permute-start = (bf16[1,560,2,840]{3,2,1,0:T(2,128)(2,1)}, bf16[1,560,2,840]{3,2,1,0:T(2,128)(2,1)}, u32[]{:S(2)}, u32[]{:S(2)}) collective-permute-start(bf16[1,560,2,840]{3,2,1,0:T(2,128)(2,1)} %bitcast.48), channel_id=1, source_target_pairs={{0,1},{1,0},{2,3},{3,2},{4,5},{5,4},{6,7},{7,6},{8,9},{9,8},{10,11... | collective-permute-start | bytes 5644808 | tf_op jit(solution)/shard_map/ppermute | solution.py:22
  59.8 7.9 %copy-start = (bf16[1,560,2,840]{3,2,1,0:T(2,128)(2,1)}, bf16[1,560,2,840]{3,2,1,0:T(2,128)(2,1)S(1)}, u32[]{:S(2)}) copy-start(bf16[1,560,2,840]{3,2,1,0:T(2,128)(2,1)S(1)} %get-tuple-element.11) | copy-start | bytes 5644804
  67.7 4.5 %copy-start.3 = (bf16[2240]{0:T(1024)(128)(2,1)S(1)}, bf16[2240]{0:T(1024)(128)(2,1)}, u32[]{:S(2)}) copy-start(bf16[2240]{0:T(1024)(128)(2,1)} %param.14) | copy-start | bytes 13444
  67.7 5.9 %copy-start.4 = (bf16[2240]{0:T(1024)(128)(2,1)S(1)}, bf16[2240]{0:T(1024)(128)(2,1)}, u32[]{:S(2)}) copy-start(bf16[2240]{0:T(1024)(128)(2,1)} %param.13) | copy-start | bytes 13444
  67.7 6.0 %copy-start.5 = (u32[32]{0:T(128)S(1)}, u32[32]{0:T(128)}, u32[]{:S(2)}) copy-start(u32[32]{0:T(128)} %constant.36) | copy-start | bytes 388
  67.7 248.6 %collective-permute-start.1 = (bf16[2,560,2,840]{3,2,1,0:T(2,128)(2,1)}, bf16[2,560,2,840]{3,2,1,0:T(2,128)(2,1)}, u32[]{:S(2)}, u32[]{:S(2)}) collective-permute-start(bf16[2,560,2,840]{3,2,1,0:T(2,128)(2,1)} %pad_maximum_fusion.1), channel_id=1, source_target_pairs={{0,2},{1,3},{2,0},{3,1},{4,6},{5,7},{6,4},{7,5},{8,10},{9,11},{10,... | collective-permute-start | bytes 11289608 | tf_op jit(solution)/shard_map/ppermute | solution.py:22
  72.0 284.2 %all-gather.2.cloned.1.call-start = ((), (), s32[]{:S(2)}) async-start(), calls=%async_computation.3 | async-start | bytes 1474560 | tf_op jit(solution)/shard_map/all_gather | solution.py:110
  316.2 99.2 %reduce-scatter.5.cloned.1.call-start = ((), (), s32[]{:S(2)}) async-start(), calls=%async_computation.4 | async-start | bytes 1474560 | tf_op jit(solution)/shard_map/reduce_scatter | solution.py:126
  356.2 13.7 %copy-start.2 = (bf16[9,2,840]{2,1,0:T(2,128)(2,1)S(1)}, bf16[9,2,840]{2,1,0:T(2,128)(2,1)}, u32[]{:S(2)}) copy-start(bf16[9,2,840]{2,1,0:T(2,128)(2,1)} %param.16) | copy-start | bytes 90724
  363.7 18.4 %collective-permute-start.3 = (bf16[4,1,64,1680]{3,2,0,1:T(8,128)(2,1)S(1)}, bf16[4,1,64,1680]{3,2,0,1:T(8,128)(2,1)S(1)}, u32[]{:S(2)}, u32[]{:S(2)}) collective-permute-start(bf16[4,1,64,1680]{3,2,0,1:T(8,128)(2,1)S(1)} %bitcast.43), channel_id=1, source_target_pairs={{1,0},{2,1},{3,2},{5,4},{6,5},{7,6},{9,8},{10,9},{11,10},{13,12},{... | collective-permute-start | bytes 2580488 | tf_op jit(solution)/shard_map/ppermute | solution.py:43
  365.0 18.3 %collective-permute-start.2 = (bf16[4,1,64,1680]{3,2,0,1:T(8,128)(2,1)S(1)}, bf16[4,1,64,1680]{3,2,0,1:T(8,128)(2,1)S(1)}, u32[]{:S(2)}, u32[]{:S(2)}) collective-permute-start(bf16[4,1,64,1680]{3,2,0,1:T(8,128)(2,1)S(1)} %bitcast.44), channel_id=1, source_target_pairs={{0,1},{1,2},{2,3},{4,5},{5,6},{6,7},{8,9},{9,10},{10,11},{12,13},{... | collective-permute-start | bytes 2580488 | tf_op jit(solution)/shard_map/ppermute | solution.py:41
  384.4 2.2 copy-start.6
  386.6 28.9 %copy-start.1 = (bf16[64,2240]{1,0:T(8,128)(2,1)S(1)}, bf16[64,2240]{1,0:T(8,128)(2,1)}, u32[]{:S(2)}) copy-start(bf16[64,2240]{1,0:T(8,128)(2,1)} %get-tuple-element.7) | copy-start | bytes 860164
Sparse Core Ops, SparseCore 0:
  72.1 100.7 reduce-scatter.2
  316.3 16.5 all-gather.1
  389.2 26.2 reduce-scatter.4
